TPU v7x, 512 devices: a whole 4x4x16 slice. The times are simulated.
512 devices in a mesh: ctx: 64 (over y, z), kvh: 8 (over x, core).
Axes of the slice: x: 4, y: 4, z: 16, core: 2. Of those that a mesh axis runs over, the one named last changes fastest.
Arguments:
- queries: bfloat16 [16384, 8192], P('ctx', 'kvh'), may hold values from -256 to 256
- keys: bfloat16 [16384, 1024], P('ctx', 'kvh'), may hold values from -4 to 4
- values: bfloat16 [16384, 1024], P('ctx', 'kvh'), may hold values from -6 to 6
- selection: int32 [8, 256, 16], P('kvh', 'ctx'), may hold values from -1 to 250, as said below
Outputs:
- attention_out: bfloat16 [16384, 8192], P(('ctx', 'kvh'))
Inputs may be any that keep to these rules, and one draw needn't show every extreme that they name: `selection`: entries -1 stand after the named tiles; the tiles of one list are distinct and each is at most b - 256 / 64 - 1 for block b. The query blocks held by one index of ctx (blocks c * 4 to (c + 1) * 4 - 1) name, together, at most 2 distinct tiles of any one other such group of blocks, and only tiles of earlier groups; some group reaches 2 in every draw.
All inputs are finite; a program needn't handle non-finite values.
Results may differ from a plain program's by a relative error of at most 0.008.
Values may be sent and summed in bfloat16 or wider, within the bound.
No kernel may reach another device: no remote copies, remote signals or barrier semaphores. Data moves between devices by JAX's collectives and lax.ppermute only.
A program may use at most 64 MiB of HBM per device.

v0:
```python
import jax
import jax.numpy as jnp
from jax import lax
from jax.sharding import PartitionSpec as P

TILE = 64
SEL = 16
WINDOW = 256
masked_score = -1e30


def passed_along(value, axis, steps):
    count = lax.axis_size(axis)
    first, last = (max(0, -steps), min(count, count - steps))
    return lax.ppermute(value, axis, [(source, source + steps) for source in range(first, last)])


def block_attention_step(
    query_rows, window_keys, window_values, window_ok, chosen_keys, chosen_values, chosen_ok, scale
):
    win_scores = (
        jnp.einsum("rhd,jd->hrj", query_rows, window_keys, preferred_element_type=jnp.float32)
        * scale
    )
    sel_scores = (
        jnp.einsum("rhd,jd->hrj", query_rows, chosen_keys, preferred_element_type=jnp.float32)
        * scale
    )
    win_scores = jnp.where(window_ok[None, :, :], win_scores, masked_score)
    sel_scores = jnp.where(chosen_ok[None, None, :], sel_scores, masked_score)
    peak = jnp.maximum(jnp.max(win_scores, axis=-1), jnp.max(sel_scores, axis=-1))
    win_weights = jnp.exp(win_scores - peak[:, :, None])
    sel_weights = jnp.exp(sel_scores - peak[:, :, None])
    total = jnp.sum(win_weights, axis=-1) + jnp.sum(sel_weights, axis=-1)
    numerator = jnp.einsum(
        "hrj,jd->rhd",
        win_weights.astype(jnp.bfloat16),
        window_values,
        preferred_element_type=jnp.float32,
    )
    numerator = numerator + jnp.einsum(
        "hrj,jd->rhd",
        sel_weights.astype(jnp.bfloat16),
        chosen_values,
        preferred_element_type=jnp.float32,
    )
    result = numerator / jnp.transpose(total)[:, :, None]
    return result.astype(jnp.bfloat16).reshape(query_rows.shape[0], -1)


def per_device(queries, keys, values, selection):
    tok_rows = queries.shape[0]
    head_size = keys.shape[1]
    per_dev = tok_rows // TILE
    here = lax.axis_index("ctx")
    scale = 1.0 / head_size**0.5
    tile_width = TILE * head_size
    flat_list = selection[0].reshape(-1)
    listed = flat_list >= 0
    safe_list = jnp.maximum(flat_list, 0)
    earlier_keys, earlier_values = passed_along((keys, values), "ctx", 1)
    window_keys = jnp.concatenate([earlier_keys, keys], axis=0)
    window_values = jnp.concatenate([earlier_values, values], axis=0)
    piece_keys = lax.all_gather(keys, "ctx", axis=0, tiled=True)
    piece_values = lax.all_gather(values, "ctx", axis=0, tiled=True)
    count = piece_keys.shape[0] // TILE
    piece_tiles = jnp.concatenate(
        [piece_keys.reshape(count, tile_width), piece_values.reshape(count, tile_width)], axis=1
    )
    picker = (safe_list[:, None] == jnp.arange(count, dtype=jnp.int32)[None, :]).astype(
        jnp.bfloat16
    )
    chosen = jnp.dot(picker, piece_tiles, preferred_element_type=jnp.float32).astype(jnp.bfloat16)
    chosen_keys = chosen[:, :tile_width].reshape(per_dev, SEL * TILE, head_size)
    chosen_values = chosen[:, tile_width:].reshape(per_dev, SEL * TILE, head_size)
    chosen_ok = jnp.repeat(listed.reshape(per_dev, SEL), TILE, axis=1)
    key_pos = here * tok_rows - tok_rows + jnp.arange(2 * tok_rows, dtype=jnp.int32)
    block_queries = queries.reshape(per_dev, TILE, -1, head_size)

    def one_block(inner):
        block_index, block_rows, block_keys, block_values, block_ok = inner
        query_pos = here * tok_rows + block_index * TILE + jnp.arange(TILE, dtype=jnp.int32)
        window_ok = (
            (key_pos[None, :] <= query_pos[:, None])
            & (key_pos[None, :] > query_pos[:, None] - WINDOW)
            & (key_pos[None, :] >= 0)
        )
        return block_attention_step(
            block_rows,
            window_keys,
            window_values,
            window_ok,
            block_keys,
            block_values,
            block_ok,
            scale,
        )

    attended = lax.map(
        one_block,
        (
            jnp.arange(per_dev, dtype=jnp.int32),
            block_queries,
            chosen_keys,
            chosen_values,
            chosen_ok,
        ),
    )
    attended = attended.reshape(tok_rows, -1)
    return lax.all_to_all(attended, "kvh", split_axis=0, concat_axis=1, tiled=True)


def solution(mesh):
    return jax.shard_map(
        per_device,
        mesh=mesh,
        in_specs=(P("ctx", "kvh"), P("ctx", "kvh"), P("ctx", "kvh"), P("kvh", "ctx", None)),
        out_specs=P(("ctx", "kvh"), None),
        check_vma=False,
    )
```

profile of v0, /device:TPU:1, one launch (start us, length us, event | category | flops | bytes accessed | tf_op | source)
XLA Modules:
  0.0 379.2 jit_solution(10833743811720009542)
XLA Ops:
  6.5 0.7 all-gather.3.cloned.1.call-update
  7.3 0.7 all-gather.5.cloned.1.call-update
  8.0 4.4 %collective-permute-start = (bf16[256,128]{1,0:T(8,128)(2,1)}, bf16[256,128]{1,0:T(8,128)(2,1)S(1)}, u32[]{:S(2)}, u32[]{:S(2)}) collective-permute-start(bf16[256,128]{1,0:T(8,128)(2,1)} %param.7), channel_id=1, source_target_pairs={{0,8},{8,16},{16,24},{24,32},{32,40},{40,48},{48,56},{56,64},{64,7... | collective-permute-start | bytes 196616 | tf_op jit(solution)/shard_map/ppermute | solution.py:15
  12.4 3.5 collective-permute-start.1
  15.9 0.7 broadcast_maximum_fusion
  16.6 0.7 compare_bitcast_fusion
  17.4 2.0 copy.42
  19.5 0.1 reshape.135
  19.6 0.9 pad_maximum_fusion
  20.4 0.9 pad_maximum_fusion.1
  21.3 132.8 %all-gather.3.cloned.1.call-done = bf16[16384,128]{1,0:T(8,128)(2,1)} async-done(((bf16[256,128]{1,0:T(8,128)(2,1)}), bf16[16384,128]{1,0:T(8,128)(2,1)}) %all-gather.3.cloned.1.call-update) | async-done | bytes 4194320 | tf_op jit(solution)/shard_map/all_gather | solution.py:64
  154.1 7.3 %reshape.136 = bf16[256,8192]{1,0:T(8,128)(2,1)} reshape(bf16[16384,128]{1,0:T(8,128)(2,1)} %all-gather.3.cloned.1.call-done) | data formatting | bytes 8388608 | tf_op jit(solution)/shard_map/reshape | solution.py:68
  161.5 136.8 %all-gather.5.cloned.1.call-done = bf16[16384,128]{1,0:T(8,128)(2,1)} async-done(((bf16[256,128]{1,0:T(8,128)(2,1)}), bf16[16384,128]{1,0:T(8,128)(2,1)}) %all-gather.5.cloned.1.call-update) | async-done | bytes 4194320 | tf_op jit(solution)/shard_map/all_gather | solution.py:65
  298.3 7.3 %reshape.137 = bf16[256,8192]{1,0:T(8,128)(2,1)} reshape(bf16[16384,128]{1,0:T(8,128)(2,1)} %all-gather.5.cloned.1.call-done) | data formatting | bytes 8388608 | tf_op jit(solution)/shard_map/reshape | solution.py:68
  305.6 5.1 %convolution_convert_fusion = bf16[64,16384]{1,0:T(8,128)(2,1)S(1)} fusion(bf16[256,8192]{1,0:T(8,128)(2,1)} %reshape.137, bf16[256,8192]{1,0:T(8,128)(2,1)} %reshape.136, s32[64]{0:T(128)S(1)} %max.21), kind=kOutput, calls=%fused_computation.43 | convolution fusion | flops 554713088 | bytes 10486016 | tf_op jit(solution)/shard_map/dot_general | solution.py:73
  310.7 0.2 fusion.35
  310.9 1.3 reshape.138
  312.2 1.3 reshape.139
  313.5 35.6 %while.13 = (s32[]{:T(128)}, bf16[4,64,1024]{2,1,0:T(8,128)(2,1)}, s32[4]{0:T(128)S(1)}, s32[]{:T(128)}, bf16[4,64,8,128]{3,2,1,0:T(8,128)(2,1)}, /*index=5*/bf1...) while((s32[]{:T(128)}, bf16[4,64,1024]{2,1,0:T(8,128)(2,1)}, ...), condition=%wide.region_5.6_spmd.clone, body=%wide.region_0.5_spmd.clone.sunk | while | flops 410321536 | bytes 14410449 | solution.py:99
  313.5 0.6 dynamic_slice.60
  314.8 0.1 and_and_fusion.2
  314.9 0.9 dynamic-slice_bitcast_fusion.2
  315.8 0.4 fusion.51
  316.3 1.5 bitcast_reduce_fusion.2
  317.8 0.5 fusion.53
  318.6 1.0 fusion.52
  319.6 1.6 convolution_bitcast_fusion.3
  321.2 0.3 fusion.54
  321.6 0.1 copy.62
  321.7 0.7 constant_dynamic-update-slice_fusion.2
  322.4 0.6 dynamic_slice.60
  323.7 0.1 and_and_fusion.2
  323.8 0.9 dynamic-slice_bitcast_fusion.2
  324.7 0.4 fusion.51
  325.2 1.5 bitcast_reduce_fusion.2
  326.7 0.5 fusion.53
  327.5 1.0 fusion.52
  328.6 1.6 convolution_bitcast_fusion.3
  330.1 0.3 fusion.54
  330.5 0.1 copy.62
  330.6 0.7 constant_dynamic-update-slice_fusion.2
  331.3 0.6 dynamic_slice.60
  332.6 0.1 and_and_fusion.2
  332.7 0.9 dynamic-slice_bitcast_fusion.2
  333.6 0.4 fusion.51
  334.2 1.5 bitcast_reduce_fusion.2
  335.6 0.5 fusion.53
  336.4 1.0 fusion.52
  337.5 1.6 convolution_bitcast_fusion.3
  339.1 0.3 fusion.54
  339.6 0.7 constant_dynamic-update-slice_fusion.2
  340.2 0.6 dynamic_slice.60
  341.5 0.1 and_and_fusion.2
  341.6 0.9 dynamic-slice_bitcast_fusion.2
  342.5 0.4 fusion.51
  343.1 1.5 bitcast_reduce_fusion.2
  344.6 0.5 fusion.53
  345.3 1.0 fusion.52
  346.4 1.6 convolution_bitcast_fusion.3
  348.0 0.3 fusion.54
  348.3 0.1 copy.62
  348.5 0.7 constant_dynamic-update-slice_fusion.2
  349.1 22.4 %all_to_all.19 = bf16[8,32,1024]{2,1,0:T(8,128)(2,1)S(1)} all-to-all(bf16[8,32,1024]{2,1,0:T(8,128)(2,1)} %bitcast.83), channel_id=1, replica_groups=mesh['ctx'=64,'kvh'=8] {'kvh'}, dimensions={0} | all-to-all | bytes 1048576 | tf_op jit(solution)/shard_map/all_to_all | solution.py:110
  371.5 0.8 copy.41
  (61 shorter events, 2.0 us)
Async XLA Ops:
  6.5 147.6 %all-gather.3.cloned.1.call-start = ((), (), s32[]{:S(2)}) async-start(), calls=%async_computation.1 | async-start | bytes 4259840 | tf_op jit(solution)/shard_map/all_gather | solution.py:64
  7.3 291.0 %all-gather.5.cloned.1.call-start = ((), (), s32[]{:S(2)}) async-start(), calls=%async_computation.2 | async-start | bytes 4259840 | tf_op jit(solution)/shard_map/all_gather | solution.py:65
  8.0 11.5 %collective-permute-start = (bf16[256,128]{1,0:T(8,128)(2,1)}, bf16[256,128]{1,0:T(8,128)(2,1)S(1)}, u32[]{:S(2)}, u32[]{:S(2)}) collective-permute-start(bf16[256,128]{1,0:T(8,128)(2,1)} %param.7), channel_id=1, source_target_pairs={{0,8},{8,16},{16,24},{24,32},{32,40},{40,48},{48,56},{56,64},{64,7... | collective-permute-start | bytes 196616 | tf_op jit(solution)/shard_map/ppermute | solution.py:15
  12.4 8.0 %collective-permute-start.1 = (bf16[256,128]{1,0:T(8,128)(2,1)}, bf16[256,128]{1,0:T(8,128)(2,1)S(1)}, u32[]{:S(2)}, u32[]{:S(2)}) collective-permute-start(bf16[256,128]{1,0:T(8,128)(2,1)} %param.8), channel_id=1, source_target_pairs={{0,8},{8,16},{16,24},{24,32},{32,40},{40,48},{48,56},{56,64},{64,7... | collective-permute-start | bytes 196616 | tf_op jit(solution)/shard_map/ppermute | solution.py:15
  319.6 1.7 copy-start
  328.5 1.7 copy-start
  337.4 1.7 copy-start
  346.3 1.7 copy-start
Sparse Core Ops, SparseCore 0:
  10.3 143.7 all-gather.2
  157.1 141.1 all-gather.4
where the time goes:
time: 380 us; the launch traced here: 379 us
  waiting for transfers between devices  271 us (71%)
  local copies, waits for them, and re-layouts  31.2 us (8%)
  blocking collectives  22.4 us (6%)
  matrix products  20.4 us (5%)
  between operations  13.5 us (4%)
  other arithmetic  9.84 us (3%)
  starting transfers between devices  7.96 us (2%)
    all_gather x1, waiting for transfers between devices, per_device(): piece_values = lax.all_gather(values, 'ctx', axis=0, tiled=True)  137 us
    all_gather x1, waiting for transfers between devices, per_device(): piece_keys = lax.all_gather(keys, 'ctx', axis=0, tiled=True)  133 us
    all_to_all x1, blocking collectives, per_device(): lax.all_to_all(attended, 'kvh', split_axis=0, concat_axis=1, tiled=True)  22.4 us
    ppermute x2, starting transfers between devices, passed_along(): lax.ppermute(value, axis, [(source, source + steps) for source in range(f...  7.92 us
  transfers between devices with their start and end apart: 4, of which 2 were waited for; matrix products, arithmetic and copies ran while one was open for 3% of the time, Pallas kernels for 0%

commit v1 on v0

--- a/solution.py
+++ b/solution.py
@@ -61,7 +61,9 @@
     earlier_keys, earlier_values = passed_along((keys, values), "ctx", 1)
     window_keys = jnp.concatenate([earlier_keys, keys], axis=0)
     window_values = jnp.concatenate([earlier_values, values], axis=0)
-    piece_keys = lax.all_gather(keys, "ctx", axis=0, tiled=True)
+    piece_keys = jnp.concatenate(
+        lax.all_to_all(jnp.stack([keys] * lax.axis_size("ctx")), "ctx", 0, 0), axis=0
+    )
     piece_values = lax.all_gather(values, "ctx", axis=0, tiled=True)
     count = piece_keys.shape[0] // TILE
     piece_tiles = jnp.concatenate(

time: 380 us -> 333 us (0.88)
  waiting for transfers between devices: 271 us -> 212 us
  starting transfers between devices: 7.96 us -> 25.7 us
  blocking collectives: 22.4 us -> 16.5 us
    ppermute x2, waiting for transfers between devices: 0.01 us -> 192 us  [passed_along(): lax.ppermute(value, axis, [(source, source + steps) for source in range(f...]
    all_gather x1 -> x0, waiting for transfers between devices: 133 us -> none  [per_device(): piece_keys = lax.all_gather(keys, 'ctx', axis=0, tiled=True)]
    all_gather x1, waiting for transfers between devices: 137 us -> 20.1 us  [per_device(): piece_values = lax.all_gather(values, 'ctx', axis=0, tiled=True)]
    all_to_all x0 -> x1, starting transfers between devices: none -> 19.7 us  [per_device(): lax.all_to_all(jnp.stack([keys] * lax.axis_size('ctx')), 'ctx', 0, 0)]
    another operation x0 -> x2, local copies, waits for them, and re-layouts: none -> 11.2 us  [the longest x1 7.34 us: per_device(): piece_keys.reshape(count, tile_width)]
    reshape x1 -> x0, local copies, waits for them, and re-layouts: 7.33 us -> none  [per_device(): piece_keys.reshape(count, tile_width)]
    all_to_all x1, blocking collectives: 22.4 us -> 16.5 us  [per_device(): lax.all_to_all(attended, 'kvh', split_axis=0, concat_axis=1, tiled=True)]
  transfers between devices with their start and end apart: 4 -> 4, of which waited for: 2 -> 3; matrix products, arithmetic and copies ran while one was open for 3% -> 3% of each run, Pallas kernels for 0% -> 0%
where the time goes in v1:
time: 333 us; the launch traced here: 332 us
  waiting for transfers between devices  212 us (64%)
  local copies, waits for them, and re-layouts  34 us (10%)
  starting transfers between devices  25.7 us (8%)
  matrix products  20.4 us (6%)
  blocking collectives  16.5 us (5%)
  between operations  13.5 us (4%)
  other arithmetic  6.8 us (2%)
    ppermute x2, waiting for transfers between devices, passed_along(): lax.ppermute(value, axis, [(source, source + steps) for source in range(f...  192 us
    all_gather x1, waiting for transfers between devices, per_device(): piece_values = lax.all_gather(values, 'ctx', axis=0, tiled=True)  20.1 us
    all_to_all x1, starting transfers between devices, per_device(): lax.all_to_all(jnp.stack([keys] * lax.axis_size('ctx')), 'ctx', 0, 0)  19.7 us
    all_to_all x1, blocking collectives, per_device(): lax.all_to_all(attended, 'kvh', split_axis=0, concat_axis=1, tiled=True)  16.5 us
    another operation x1, local copies, waits for them, and re-layouts, per_device(): piece_keys.reshape(count, tile_width)  7.34 us
    reshape x1, local copies, waits for them, and re-layouts, per_device(): piece_values.reshape(count, tile_width)  7.31 us
  transfers between devices with their start and end apart: 4, of which 3 were waited for; matrix products, arithmetic and copies ran while one was open for 3% of the time, Pallas kernels for 0%

profile of v1, /device:TPU:1, one launch (start us, length us, event | category | flops | bytes accessed | tf_op | source)
XLA Modules:
  0.0 332.2 jit_solution(14544985331312795942)
XLA Ops:
  6.5 3.8 %stack.2 = bf16[64,256,128]{2,1,0:T(8,128)(2,1)} broadcast(bf16[256,128]{1,0:T(8,128)(2,1)} %param.7), dimensions={1,2} | broadcast | bytes 4259840 | tf_op jit(solution)/shard_map/stack | solution.py:65
  10.4 19.7 %all-to-all-start = ((bf16[64,256,128]{2,1,0:T(8,128)(2,1)}), bf16[64,256,128]{2,1,0:T(8,128)(2,1)}, u32[]{:S(2)}, u32[]{:S(2)}) async-start(bf16[64,256,128]{2,1,0:T(8,128)(2,1)} %stack.2), calls=%async_computation | async-start | bytes 8388608 | tf_op jit(solution)/shard_map/all_to_all | solution.py:65
  30.1 0.7 all-gather.2.cloned.1.call-update
  30.8 2.8 collective-permute-start
  33.7 3.1 collective-permute-start.1
  36.9 0.9 copy.42
  37.9 0.1 reshape.134
  38.0 186.6 %collective-permute-done = bf16[256,128]{1,0:T(8,128)(2,1)S(1)} collective-permute-done((bf16[256,128]{1,0:T(8,128)(2,1)S(1)}, bf16[256,128]{1,0:T(8,128)(2,1)S(1)}, u32[]{:S(2)}, u32[]{:S(2)}) %collective-permute-start) | collective-permute-done | bytes 65568 | tf_op jit(solution)/shard_map/ppermute | solution.py:15
  224.6 5.1 %collective-permute-done.1 = bf16[256,128]{1,0:T(8,128)(2,1)S(1)} collective-permute-done((bf16[256,128]{1,0:T(8,128)(2,1)S(1)}, bf16[256,128]{1,0:T(8,128)(2,1)S(1)}, u32[]{:S(2)}, u32[]{:S(2)}) %collective-permute-start.1) | collective-permute-done | bytes 65568 | tf_op jit(solution)/shard_map/ppermute | solution.py:15
  229.6 20.1 %all-gather.2.cloned.1.call-done = bf16[16384,128]{1,0:T(8,128)(2,1)} async-done(((bf16[256,128]{1,0:T(8,128)(2,1)}), bf16[16384,128]{1,0:T(8,128)(2,1)}) %all-gather.2.cloned.1.call-update) | async-done | bytes 4194320 | tf_op jit(solution)/shard_map/all_gather | solution.py:67
  249.7 7.3 %reshape.135 = bf16[256,8192]{1,0:T(8,128)(2,1)} reshape(bf16[16384,128]{1,0:T(8,128)(2,1)} %all-gather.2.cloned.1.call-done) | data formatting | bytes 8388608 | tf_op jit(solution)/shard_map/reshape | solution.py:70
  257.1 7.3 %reshape_reshape.3 = bf16[256,8192]{1,0:T(8,128)(2,1)} reshape(bf16[64,256,128]{2,1,0:T(8,128)(2,1)} %all-to-all-done) | data formatting | bytes 8388608 | tf_op jit(solution)/shard_map/reshape;reshape | solution.py:70
  264.4 5.1 %convolution_convert_fusion = bf16[64,16384]{1,0:T(8,128)(2,1)S(1)} fusion(bf16[256,8192]{1,0:T(8,128)(2,1)} %reshape.135, bf16[256,8192]{1,0:T(8,128)(2,1)} %reshape_reshape.3, s32[64]{0:T(128)S(1)} %max.21), kind=kOutput, calls=%fused_computation.43 | convolution fusion | flops 554713088 | bytes 10486016 | tf_op jit(solution)/shard_map/dot_general | solution.py:75
  269.5 0.2 fusion.35
  269.7 1.3 reshape.136
  271.0 1.3 reshape.137
  272.2 35.8 %while.13 = (s32[]{:T(128)}, bf16[4,64,1024]{2,1,0:T(8,128)(2,1)}, s32[4]{0:T(128)S(1)}, s32[]{:T(128)}, bf16[4,64,8,128]{3,2,1,0:T(8,128)(2,1)}, /*index=5*/bf1...) while((s32[]{:T(128)}, bf16[4,64,1024]{2,1,0:T(8,128)(2,1)}, ...), condition=%wide.region_5.6_spmd.clone, body=%wide.region_0.5_spmd.clone.sunk | while | flops 410321536 | bytes 14410449 | solution.py:101
  272.2 0.6 dynamic_slice.60
  273.6 0.1 and_and_fusion.2
  273.7 0.9 dynamic-slice_bitcast_fusion.2
  274.6 0.4 fusion.51
  275.1 1.5 bitcast_reduce_fusion.2
  276.6 0.5 fusion.53
  277.2 0.1 copy.60
  277.3 1.0 fusion.52
  278.4 1.6 convolution_bitcast_fusion.3
  280.0 0.3 fusion.54
  280.4 0.1 copy.62
  280.5 0.7 constant_dynamic-update-slice_fusion.2
  281.2 0.6 dynamic_slice.60
  282.5 0.1 and_and_fusion.2
  282.6 0.9 dynamic-slice_bitcast_fusion.2
  283.5 0.4 fusion.51
  284.1 1.5 bitcast_reduce_fusion.2
  285.6 0.5 fusion.53
  286.3 1.0 fusion.52
  287.4 1.6 convolution_bitcast_fusion.3
  289.0 0.3 fusion.54
  289.3 0.1 copy.62
  289.5 0.7 constant_dynamic-update-slice_fusion.2
  290.1 0.6 dynamic_slice.60
  291.4 0.1 and_and_fusion.2
  291.5 0.9 dynamic-slice_bitcast_fusion.2
  292.5 0.4 fusion.51
  293.0 1.5 bitcast_reduce_fusion.2
  294.5 0.5 fusion.53
  295.2 1.0 fusion.52
  296.3 1.6 convolution_bitcast_fusion.3
  297.9 0.3 fusion.54
  298.2 0.1 copy.62
  298.4 0.7 constant_dynamic-update-slice_fusion.2
  299.1 0.6 dynamic_slice.60
  300.4 0.1 and_and_fusion.2
  300.5 0.9 dynamic-slice_bitcast_fusion.2
  301.4 0.4 fusion.51
  301.9 1.5 bitcast_reduce_fusion.2
  303.4 0.5 fusion.53
  304.2 1.0 fusion.52
  305.3 1.6 convolution_bitcast_fusion.3
  306.9 0.3 fusion.54
  307.2 0.1 copy.62
  307.4 0.7 constant_dynamic-update-slice_fusion.2
  308.0 16.5 %all_to_all.24 = bf16[8,32,1024]{2,1,0:T(8,128)(2,1)S(1)} all-to-all(bf16[8,32,1024]{2,1,0:T(8,128)(2,1)} %bitcast.83), channel_id=1, replica_groups=mesh['ctx'=64,'kvh'=8] {'kvh'}, dimensions={0} | all-to-all | bytes 1048576 | tf_op jit(solution)/shard_map/all_to_all | solution.py:112
  324.5 0.8 copy.41
  (69 shorter events, 1.8 us)
Async XLA Ops:
  10.4 20.4 %copy-start.2 = (bf16[256,128]{1,0:T(8,128)(2,1)S(1)}, bf16[256,128]{1,0:T(8,128)(2,1)}, u32[]{:S(2)}) copy-start(bf16[256,128]{1,0:T(8,128)(2,1)} %param.7) | copy-start | bytes 196612
  10.4 23.3 %copy-start.3 = (bf16[256,128]{1,0:T(8,128)(2,1)S(1)}, bf16[256,128]{1,0:T(8,128)(2,1)}, u32[]{:S(2)}) copy-start(bf16[256,128]{1,0:T(8,128)(2,1)} %param.8) | copy-start | bytes 196612
  10.4 26.4 %copy-start.4 = (s32[1,4,16]{2,1,0:T(4,128)S(1)}, s32[1,4,16]{2,1,0:T(4,128)}, u32[]{:S(2)}) copy-start(s32[1,4,16]{2,1,0:T(4,128)} %param.9) | copy-start | bytes 772
  10.4 26.5 %copy-start.1 = (bf16[256,1024]{1,0:T(8,128)(2,1)S(1)}, bf16[256,1024]{1,0:T(8,128)(2,1)}, u32[]{:S(2)}) copy-start(bf16[256,1024]{1,0:T(8,128)(2,1)} %param.6) | copy-start | bytes 1572868
  10.4 246.7 %all-to-all-start = ((bf16[64,256,128]{2,1,0:T(8,128)(2,1)}), bf16[64,256,128]{2,1,0:T(8,128)(2,1)}, u32[]{:S(2)}, u32[]{:S(2)}) async-start(bf16[64,256,128]{2,1,0:T(8,128)(2,1)} %stack.2), calls=%async_computation | async-start | bytes 8388608 | tf_op jit(solution)/shard_map/all_to_all | solution.py:65
  30.1 219.7 %all-gather.2.cloned.1.call-start = ((), (), s32[]{:S(2)}) async-start(), calls=%async_computation.2 | async-start | bytes 4259840 | tf_op jit(solution)/shard_map/all_gather | solution.py:67
  30.8 193.7 %collective-permute-start = (bf16[256,128]{1,0:T(8,128)(2,1)S(1)}, bf16[256,128]{1,0:T(8,128)(2,1)S(1)}, u32[]{:S(2)}, u32[]{:S(2)}) collective-permute-start(bf16[256,128]{1,0:T(8,128)(2,1)S(1)} %copy-done.2), channel_id=1, source_target_pairs={{0,8},{8,16},{16,24},{24,32},{32,40},{40,48},{48,56},{56,64},{64,7... | collective-permute-start | bytes 196616 | tf_op jit(solution)/shard_map/ppermute | solution.py:15
  33.7 195.9 %collective-permute-start.1 = (bf16[256,128]{1,0:T(8,128)(2,1)S(1)}, bf16[256,128]{1,0:T(8,128)(2,1)S(1)}, u32[]{:S(2)}, u32[]{:S(2)}) collective-permute-start(bf16[256,128]{1,0:T(8,128)(2,1)S(1)} %copy-done.3), channel_id=1, source_target_pairs={{0,8},{8,16},{16,24},{24,32},{32,40},{40,48},{48,56},{56,64},{64,7... | collective-permute-start | bytes 196616 | tf_op jit(solution)/shard_map/ppermute | solution.py:15
  278.4 1.7 copy-start
  287.3 1.7 copy-start
  296.2 1.7 copy-start
  305.2 1.7 copy-start
Sparse Core Ops, SparseCore 0:
  33.8 215.8 all-gather.1
